TPU v7x, 256 devices: a whole 4x4x8 slice. The times are simulated.
256 devices in a mesh: seq: 64 (over x, z_lo, y, core), mp: 4 (over z_hi).
Axes of the slice: x: 4, y: 4, z: 8 (z_hi: 4, z_lo: 2; z = z_hi * 2 + z_lo), core: 2. Of those that a mesh axis runs over, the one named last changes fastest.
Arguments:
- tokens: bfloat16 [8192, 4096], P('seq', 'mp'), may hold values from -6 to 6
- w_proj: bfloat16 [4096, 3, 2048], P('seq', None, 'mp'), may hold values from -0.09375 to 0.09375
- short_filter: float32 [3, 3, 2048], P(None, None, 'mp'), may hold values from -3.5 to 3.5
- long_filter: float32 [2048, 8192], P(('mp', 'seq')), may hold values from -0.0625 to 0.0625
- skip_gain: float32 [2048], P('mp'), may hold values from -4 to 4
Outputs:
- gated: bfloat16 [8192, 2048], P('seq', 'mp')
All inputs are finite; a program needn't handle non-finite values.
Results may differ from a plain program's by a relative error of at most 0.012.
Values may be sent and summed in bfloat16 or wider, within the bound.
No kernel may reach another device: no remote copies, remote signals or barrier semaphores. Data moves between devices by JAX's collectives and lax.ppermute only.
A program may use at most 64 MiB of HBM per device.

v0:
```python
import math
import jax
import jax.numpy as jnp
from jax import lax
from jax.sharding import PartitionSpec as P


def shifted(value, axis, steps):
    count = lax.axis_size(axis)
    leading, last = (max(0, -steps), min(count, count - steps))
    return lax.ppermute(value, axis, [(source, source + steps) for source in range(leading, last)])


def transform(real_part, imag_part, orient, filled):
    length = real_part.shape[-1]
    first = math.gcd(length, 64)
    highest = lax.Precision.HIGHEST
    if length <= 64 or first == 1:
        counter = jnp.arange(length, dtype=jnp.int32)
        angles = (
            2.0
            * math.pi
            / length
            * (counter[:, None] * counter[None, :] % length).astype(jnp.float32)
        )
        cosine = jnp.cos(angles)
        sine = jnp.sin(angles)
        new_real = jnp.dot(real_part, cosine, precision=highest) - orient * jnp.dot(
            imag_part, sine, precision=highest
        )
        new_imag = jnp.dot(imag_part, cosine, precision=highest) + orient * jnp.dot(
            real_part, sine, precision=highest
        )
        return (new_real, new_imag)
    second = length // first
    outer = real_part.shape[:-1]
    live = first
    if filled > 0 and filled % second == 0:
        live = filled // second
    real_grid = real_part.reshape(outer + (first, second))[..., :live, :]
    imag_grid = imag_part.reshape(outer + (first, second))[..., :live, :]
    counter = jnp.arange(first, dtype=jnp.int32)
    angles = (
        2.0 * math.pi / first * (counter[:, None] * counter[None, :] % first).astype(jnp.float32)
    )
    cosine = jnp.cos(angles)[:live]
    sine = jnp.sin(angles)[:live]
    section_real = jnp.einsum(
        "...ab,ak->...kb", real_grid, cosine, precision=highest
    ) - orient * jnp.einsum("...ab,ak->...kb", imag_grid, sine, precision=highest)
    section_imag = jnp.einsum(
        "...ab,ak->...kb", imag_grid, cosine, precision=highest
    ) + orient * jnp.einsum("...ab,ak->...kb", real_grid, sine, precision=highest)
    freq_rows = jnp.arange(first, dtype=jnp.int32)[:, None]
    time_cols = jnp.arange(second, dtype=jnp.int32)[None, :]
    twiddle = 2.0 * math.pi / length * (freq_rows * time_cols).astype(jnp.float32)
    twist_cos = jnp.cos(twiddle)
    twist_sin = jnp.sin(twiddle)
    turned_real = section_real * twist_cos - orient * section_imag * twist_sin
    turned_imag = section_imag * twist_cos + orient * section_real * twist_sin
    inner_real, inner_imag = transform(turned_real, turned_imag, orient, 0)
    final_real = jnp.swapaxes(inner_real, -1, -2).reshape(outer + (length,))
    final_imag = jnp.swapaxes(inner_imag, -1, -2).reshape(outer + (length,))
    return (final_real, final_imag)


def mirrored(values):
    return jnp.concatenate([values[:, :1], values[:, :0:-1]], axis=1)


def long_conv(signal, kernel):
    seq_len = signal.shape[-1]
    padded_signal = jnp.pad(signal.astype(jnp.float32), ((0, 0), (0, seq_len)))
    padded_kernel = jnp.pad(kernel, ((0, 0), (0, seq_len)))
    joint_real, joint_imag = transform(padded_signal, padded_kernel, -1.0, seq_len)
    mirror_real = mirrored(joint_real)
    mirror_imag = mirrored(joint_imag)
    signal_real = 0.5 * (joint_real + mirror_real)
    signal_imag = 0.5 * (joint_imag - mirror_imag)
    kernel_real = 0.5 * (joint_imag + mirror_imag)
    kernel_imag = -0.5 * (joint_real - mirror_real)
    prod_real = signal_real * kernel_real - signal_imag * kernel_imag
    prod_imag = signal_real * kernel_imag + signal_imag * kernel_real
    back_real, back_imag = transform(prod_real, prod_imag, 1.0, 0)
    return back_real[:, :seq_len] / (2.0 * seq_len)


def on_device(tokens, w_proj, short_filter, long_filter, skip_gain):
    rows_dev = tokens.shape[0]
    margin = short_filter.shape[1] - 1
    width = w_proj.shape[2]
    source = lax.all_gather(tokens, "mp", axis=1, tiled=True)
    projected = jnp.einsum(
        "td,dpc->tpc",
        source,
        lax.all_gather(w_proj, "seq", axis=0, tiled=True),
        preferred_element_type=jnp.float32,
    ).astype(jnp.bfloat16)
    tail = shifted(projected[rows_dev - margin :], "seq", 1)
    extended = jnp.concatenate([tail, projected], axis=0).astype(jnp.float32)
    mixed = jnp.zeros((rows_dev, 3, width), jnp.float32)
    for offset in range(margin + 1):
        mixed = (
            mixed
            + short_filter[:, offset, :][None]
            * extended[margin - offset : margin - offset + rows_dev]
        )
    query_rows = mixed[:, 0]
    product = (mixed[:, 1] * mixed[:, 2]).astype(jnp.bfloat16)
    groups = lax.axis_size("seq")
    channel_count = width // groups
    outgoing = product.reshape(rows_dev, groups, channel_count).transpose(1, 2, 0)
    arrived = lax.all_to_all(outgoing, "seq", split_axis=0, concat_axis=2, tiled=True)[0]
    convolved = long_conv(arrived, long_filter).astype(jnp.bfloat16)[None]
    returned = lax.all_to_all(convolved, "seq", split_axis=2, concat_axis=0, tiled=True)
    back_rows = returned.transpose(2, 0, 1).reshape(rows_dev, width)
    result = query_rows * (
        back_rows.astype(jnp.float32) + skip_gain[None, :] * product.astype(jnp.float32)
    )
    return result.astype(jnp.bfloat16)


def solution(mesh):
    return jax.shard_map(
        on_device,
        mesh=mesh,
        in_specs=(
            P("seq", "mp"),
            P("seq", None, "mp"),
            P(None, None, "mp"),
            P(("mp", "seq"), None),
            P("mp"),
        ),
        out_specs=P("seq", "mp"),
        check_vma=False,
    )
```

profile of v0, /device:TPU:1, one launch (start us, length us, event | category | flops | bytes accessed | tf_op | source)
XLA Modules:
  0.0 374.8 jit_solution(6726618726081883636)
XLA Ops:
  6.5 0.7 all-gather.3.cloned.1.call-update
  7.3 0.7 all-gather.5.cloned.1.call-update
  8.8 0.9 fusion.158
  9.7 37.3 %all-gather.3.cloned.1.call-done = bf16[128,4096]{1,0:T(8,128)(2,1)} async-done(((bf16[128,1024]{1,0:T(8,128)(2,1)}), bf16[128,4096]{1,0:T(8,128)(2,1)}) %all-gather.3.cloned.1.call-update) | async-done | bytes 1048592 | tf_op jit(solution)/shard_map/all_gather | solution.py:92
  47.0 120.2 %all-gather.5.cloned.1.call-done = bf16[4096,3,512]{2,0,1:T(8,128)(2,1)} async-done(((bf16[64,3,512]{2,0,1:T(8,128)(2,1)}), bf16[4096,3,512]{2,0,1:T(8,128)(2,1)}) %all-gather.5.cloned.1.call-update) | async-done | bytes 12582928 | tf_op jit(solution)/shard_map/all_gather | solution.py:96
  167.2 6.7 %convolution_convert_fusion = bf16[128,3,512]{2,0,1:T(8,128)(2,1)S(1)} fusion(bf16[4096,3,512]{2,0,1:T(8,128)(2,1)} %all-gather.5.cloned.1.call-done, bf16[128,4096]{1,0:T(8,128)(2,1)} %all-gather.3.cloned.1.call-done), kind=kOutput, calls=%fused_computation.14 | convolution fusion | flops 1610809344 | bytes 14024704 | tf_op jit(solution)/shard_map/td,dpc->tpc/dot_general | solution.py:93
  173.9 2.8 collective-permute-start
  177.9 0.9 copy-done
  178.8 0.8 copy.108
  179.5 8.7 %all-to-all-start = ((bf16[64,8,128]{2,1,0:T(8,128)(2,1)}), bf16[64,8,128]{2,1,0:T(8,128)(2,1)S(1)}, u32[]{:S(2)}, u32[]{:S(2)}) async-start(bf16[64,8,128]{2,1,0:T(8,128)(2,1)} %bitcast.7), calls=%async_computation | async-start | bytes 262144 | tf_op jit(solution)/shard_map/all_to_all | solution.py:113
  189.1 7.4 %all-to-all-done = bf16[64,8,128]{2,1,0:T(8,128)(2,1)S(1)} async-done(((bf16[64,8,128]{2,1,0:T(8,128)(2,1)}), bf16[64,8,128]{2,1,0:T(8,128)(2,1)S(1)}, u32[]{:S(2)}, u32[]{:S(2)}) %all-to-all-start) | async-done | bytes 131104 | tf_op jit(solution)/shard_map/all_to_all | solution.py:113
  199.3 3.3 fusion.41
  202.6 1.4 copy.109
  203.9 1.8 copy.111
  205.7 3.3 fusion.43
  209.0 3.3 fusion.5
  212.3 4.7 %add_bitcast_fusion.1 = (f32[8,64,64,4]{1,2,3,0:T(8,128)}, f32[8,64,64,4]{1,2,3,0:T(8,128)S(1)}) fusion(f32[64,8,64,4]{2,0,3,1:T(8,128)S(1)} %fusion.5, f32[64,4]{0,1:T(4,128)S(1)} %get-tuple-element.23, f32[64,4]{0,1:T(4,128)S(1)} %get-tuple-element.22, f32[64,8,64,4]{2,0,3,1:T(8,128)S(1)} %fusion.43, f32[8,64,64,4]{2,1,3,0:T(8,128)S(1)} %copy.114), kind=kOutput, calls=%fused_computation.24 | convolution fusion | flops 101769216 | bytes 2623488 | tf_op jit(solution)/shard_map/...ab,ak->...kb/dot_general | solution.py:50
  217.3 1.9 fusion.74
  219.3 1.6 copy.120
  220.9 3.1 fusion.4
  223.9 1.5 copy.166
  225.5 1.1 reshape.129
  226.6 1.2 reshape.130
  227.8 1.3 slice.96
  229.1 1.9 fusion.72
  231.0 2.1 fusion.2
  234.4 8.9 %reverse = f32[8,16384]{1,0:T(8,128)S(1)} reverse(f32[8,16384]{1,0:T(8,128)S(1)} %bitcast.226), dimensions={1} | reverse | bytes 1048576
  243.5 9.3 %reverse.1 = f32[8,16384]{1,0:T(8,128)S(1)} reverse(f32[8,16384]{1,0:T(8,128)S(1)} %bitcast.229), dimensions={1} | reverse | bytes 1048576
  253.9 0.8 fusion.35
  254.6 0.8 fusion.37
  255.4 0.8 convolution_add_fusion.2
  256.2 0.9 subtract_bitcast_fusion.2
  258.1 3.3 fusion.39
  261.4 1.4 copy.129
  262.8 1.8 copy.131
  264.5 3.3 fusion.45
  267.8 3.3 convolution_add_fusion
  271.1 4.6 %add_bitcast_fusion = (f32[8,64,64,4]{1,2,3,0:T(8,128)S(1)}, f32[8,64,64,4]{1,2,3,0:T(8,128)}) fusion(f32[64,8,64,4]{2,0,3,1:T(8,128)S(1)} %convolution_add_fusion, f32[64,4]{0,1:T(4,128)S(1)} %fusion.76, f32[64,4]{0,1:T(4,128)S(1)} %get-tuple-element.22, f32[64,8,64,4]{2,0,3,1:T(8,128)S(1)} %fusion.45, f32[8,64,64,4]{2,1,3,0:T(8,128)S(1)} %copy.134), kind=kOutput, calls=%fused_computation.22 | convolution fusion | flops 101638144 | bytes 2623488 | tf_op jit(solution)/shard_map/...ab,ak->...kb/dot_general | solution.py:50
  275.7 1.6 copy.139
  277.4 1.9 fusion.70
  279.7 2.0 fusion
  282.4 6.8 %copy.142 = bf16[1,8,8192]{1,0,2:T(2,128)(2,1)} copy(bf16[1,8,8192]{2,1,0:T(8,128)(2,1)S(1)} %fusion.21) | data formatting | bytes 262144 | tf_op jit(solution)/shard_map/broadcast_in_dim | solution.py:114
  289.7 45.4 %reduce = bf16[8192,8]{1,0:T(8,128)(2,1)S(1)} reduce(bf16[8192,1,8]{2,1,0:T(2,128)(2,1)} %bitcast.215, bf16[]{:T(256)} %broadcast.303), dimensions={1}, to_apply=%bitcast.180.reduce_sub_computation | reduce | bytes 262146
  335.1 2.3 reshape.159
  337.4 12.7 %all_to_all.21 = bf16[64,2,512]{2,1,0:T(2,128)(2,1)S(1)} all-to-all(bf16[64,2,512]{2,1,0:T(2,128)(2,1)S(1)} %reshape.159), channel_id=1, replica_groups=mesh['seq'=64,'mp'=4] {'seq'}, dimensions={0} | all-to-all | bytes 262144 | tf_op jit(solution)/shard_map/all_to_all | solution.py:115
  350.1 8.7 %reshape.160 = bf16[8192,1,8]{2,1,0:T(2,128)(2,1)} reshape(bf16[64,2,512]{2,1,0:T(2,128)(2,1)S(1)} %all_to_all.21) | data formatting | bytes 262144
  358.8 7.8 %copy.143 = bf16[1,8,8192]{2,1,0:T(8,128)(2,1)S(1)} copy(bf16[1,8,8192]{1,0,2:T(2,128)(2,1)} %bitcast.216) | data formatting | bytes 262144 | tf_op jit(solution)/shard_map/all_to_all | solution.py:115
  367.0 0.7 fusion.17
  (58 shorter events, 11.5 us)
Async XLA Ops:
  6.5 181.7 %copy-start.3 = (f32[8,8192]{1,0:T(8,128)S(1)}, f32[8,8192]{1,0:T(8,128)}, u32[]{:S(2)}) copy-start(f32[8,8192]{1,0:T(8,128)} %param.8) | copy-start | bytes 786436
  6.5 40.4 %all-gather.3.cloned.1.call-start = ((), (), s32[]{:S(2)}) async-start(), calls=%async_computation.2 | async-start | bytes 1310720 | tf_op jit(solution)/shard_map/all_gather | solution.py:92
  7.3 159.9 %all-gather.5.cloned.1.call-start = ((), (), s32[]{:S(2)}) async-start(), calls=%async_computation.3 | async-start | bytes 12779520 | tf_op jit(solution)/shard_map/all_gather | solution.py:96
  173.9 3.6 collective-permute-start
  177.8 0.9 copy-start
  179.5 17.0 %all-to-all-start = ((bf16[64,8,128]{2,1,0:T(8,128)(2,1)}), bf16[64,8,128]{2,1,0:T(8,128)(2,1)S(1)}, u32[]{:S(2)}, u32[]{:S(2)}) async-start(bf16[64,8,128]{2,1,0:T(8,128)(2,1)} %bitcast.7), calls=%async_computation | async-start | bytes 262144 | tf_op jit(solution)/shard_map/all_to_all | solution.py:113
  227.8 25.2 %slice-start = ((f32[8,16384]{1,0:T(8,128)}), f32[8,1]{1,0:T(8,128)S(1)}, s32[]{:S(2)}) async-start(f32[8,16384]{1,0:T(8,128)} %reshape.130), calls=%async_computation.4 | async-start | bytes 8192 | tf_op jit(solution)/shard_map/slice | solution.py:68
  227.8 25.6 %copy-start.2 = (f32[8,64,256]{2,1,0:T(8,128)S(1)}, f32[8,64,256]{2,1,0:T(8,128)}, u32[]{:S(2)}) copy-start(f32[8,64,256]{2,1,0:T(8,128)} %reshape.129) | copy-start | bytes 1572868
  282.0 85.0 %copy-start.1 = (f32[128,3,512]{2,0,1:T(8,128)S(1)}, f32[128,3,512]{2,0,1:T(8,128)}, u32[]{:S(2)}) copy-start(f32[128,3,512]{2,0,1:T(8,128)} %copy-done) | copy-start | bytes 2359300
  282.0 85.0 %copy-start.4 = (f32[512]{0:T(512)S(1)}, f32[512]{0:T(512)}, u32[]{:S(2)}) copy-start(f32[512]{0:T(512)} %param.9) | copy-start | bytes 6148
Sparse Core Ops, SparseCore 0:
  9.1 37.7 all-gather.2
  48.8 118.2 all-gather.4
where the time goes:
time: 379 us; the launch traced here: 375 us
  waiting for transfers between devices  167 us (44%)
  local copies, waits for them, and re-layouts  67.2 us (18%)
  matrix products  54 us (14%)
  other arithmetic  48.3 us (13%)
  between operations  14.1 us (4%)
  blocking collectives  12.7 us (3%)
  starting transfers between devices  11.5 us (3%)
    all_gather x1, waiting for transfers between devices, on_device(): lax.all_gather(w_proj, 'seq', axis=0, tiled=True)  120 us
    unnamed x2, other arithmetic  45.4 us
    all_gather x1, waiting for transfers between devices, on_device(): source = lax.all_gather(tokens, 'mp', axis=1, tiled=True)  37.3 us
    unnamed x22, local copies, waits for them, and re-layouts  31.3 us
    all_to_all x1, blocking collectives, on_device(): lax.all_to_all(convolved, 'seq', split_axis=2, concat_axis=0, tiled=True)  12.7 us
    dot_general x4, matrix products, transform(): jnp.einsum('...ab,ak->...kb', imag_grid, sine, precision=highest)  10.8 us
    all_to_all x1, starting transfers between devices, on_device(): lax.all_to_all(outgoing, 'seq', split_axis=0, concat_axis=2, tiled=True)[0]  8.66 us
    dot_general x4, matrix products, transform(): jnp.einsum('...ab,ak->...kb', imag_grid, cosine, precision=highest)  7.92 us
  transfers between devices with their start and end apart: 4, of which 4 were waited for; matrix products, arithmetic and copies ran while one was open for 1% of the time, Pallas kernels for 0%

commit v1 on v0

--- a/solution.py
+++ b/solution.py
@@ -89,7 +89,10 @@
     rows_dev = tokens.shape[0]
     margin = short_filter.shape[1] - 1
     width = w_proj.shape[2]
-    source = lax.all_gather(tokens, "mp", axis=1, tiled=True)
+    views = []
+    for _ in range(lax.psum(1, "mp")):
+        views.append(tokens)
+    source = jnp.concatenate(lax.all_to_all(jnp.stack(views, 0), "mp", 0, 0), 1)
     projected = jnp.einsum(
         "td,dpc->tpc",
         source,

time: 379 us -> 355 us (0.937)
  waiting for transfers between devices: 167 us -> 129 us
  starting transfers between devices: 11.5 us -> 20.6 us
    all_gather x1 -> x0, waiting for transfers between devices: 37.3 us -> none  [on_device(): source = lax.all_gather(tokens, 'mp', axis=1, tiled=True)]
    all_to_all x0 -> x1, waiting for transfers between devices: none -> 29.7 us  [on_device(): source = jnp.concatenate(lax.all_to_all(jnp.stack(views, 0), 'mp', 0, 0), 1)]
    all_gather x1, waiting for transfers between devices: 120 us -> 90.9 us  [on_device(): lax.all_gather(w_proj, 'seq', axis=0, tiled=True)]
    all_to_all x0 -> x1, starting transfers between devices: none -> 9 us  [on_device(): source = jnp.concatenate(lax.all_to_all(jnp.stack(views, 0), 'mp', 0, 0), 1)]
  transfers between devices with their start and end apart: 4 -> 4, of which waited for: 4 -> 4; matrix products, arithmetic and copies ran while one was open for 1% -> 2% of each run, Pallas kernels for 0% -> 0%
where the time goes in v1:
time: 355 us; the launch traced here: 350 us
  waiting for transfers between devices  129 us (36%)
  local copies, waits for them, and re-layouts  70.8 us (20%)
  matrix products  53.6 us (15%)
  other arithmetic  48.3 us (14%)
  starting transfers between devices  20.6 us (6%)
  between operations  14.1 us (4%)
  blocking collectives  12.7 us (4%)
    all_gather x1, waiting for transfers between devices, on_device(): lax.all_gather(w_proj, 'seq', axis=0, tiled=True)  90.9 us
    unnamed x2, other arithmetic  45.4 us
    unnamed x22, local copies, waits for them, and re-layouts  31.2 us
    all_to_all x1, waiting for transfers between devices, on_device(): source = jnp.concatenate(lax.all_to_all(jnp.stack(views, 0), 'mp', 0, 0), 1)  29.7 us
    all_to_all x1, blocking collectives, on_device(): lax.all_to_all(convolved, 'seq', split_axis=2, concat_axis=0, tiled=True)  12.7 us
    dot_general x4, matrix products, transform(): jnp.einsum('...ab,ak->...kb', imag_grid, sine, precision=highest)  10.8 us
    all_to_all x1, starting transfers between devices, on_device(): source = jnp.concatenate(lax.all_to_all(jnp.stack(views, 0), 'mp', 0, 0), 1)  9 us
    all_to_all x1, starting transfers between devices, on_device(): lax.all_to_all(outgoing, 'seq', split_axis=0, concat_axis=2, tiled=True)[0]  8.84 us
  transfers between devices with their start and end apart: 4, of which 4 were waited for; matrix products, arithmetic and copies ran while one was open for 2% of the time, Pallas kernels for 0%

profile of v1, /device:TPU:1, one launch (start us, length us, event | category | flops | bytes accessed | tf_op | source)
XLA Modules:
  0.0 349.5 jit_solution(3642615324121616489)
XLA Ops:
  7.3 2.1 stack.2
  9.4 9.0 %all-to-all-start = ((bf16[4,128,1024]{2,1,0:T(8,128)(2,1)}), bf16[4,128,1024]{2,1,0:T(8,128)(2,1)S(1)}, u32[]{:S(2)}, u32[]{:S(2)}) async-start(bf16[4,128,1024]{2,1,0:T(8,128)(2,1)} %stack.2), calls=%async_computation | async-start | bytes 2097152 | tf_op jit(solution)/shard_map/all_to_all | solution.py:95
  19.2 0.9 fusion.157
  20.0 29.7 %all-to-all-done = bf16[4,128,1024]{2,1,0:T(8,128)(2,1)S(1)} async-done(((bf16[4,128,1024]{2,1,0:T(8,128)(2,1)}), bf16[4,128,1024]{2,1,0:T(8,128)(2,1)S(1)}, u32[]{:S(2)}, u32[]{:S(2)}) %all-to-all-start) | async-done | bytes 1048608 | tf_op jit(solution)/shard_map/all_to_all | solution.py:95
  49.7 0.8 copy.109
  50.5 0.8 reshape.152
  51.3 90.9 %all-gather.2.cloned.1.call-done = bf16[4096,3,512]{2,0,1:T(8,128)(2,1)} async-done(((bf16[64,3,512]{2,0,1:T(8,128)(2,1)}), bf16[4096,3,512]{2,0,1:T(8,128)(2,1)}) %all-gather.2.cloned.1.call-update) | async-done | bytes 12582928 | tf_op jit(solution)/shard_map/all_gather | solution.py:99
  142.2 6.4 %convolution_convert_fusion = bf16[128,3,512]{2,0,1:T(8,128)(2,1)S(1)} fusion(bf16[128,4096,1]{1,0,2:T(8,128)(2,1)S(1)} %reshape.152, bf16[4096,3,512]{2,0,1:T(8,128)(2,1)} %all-gather.2.cloned.1.call-done), kind=kOutput, calls=%fused_computation.14 | convolution fusion | flops 1610809344 | bytes 14024704 | tf_op jit(solution)/shard_map/td,dpc->tpc/dot_general | solution.py:96
  148.6 2.8 collective-permute-start
  152.5 0.9 copy-done
  153.4 0.8 copy.110
  154.2 8.8 %all-to-all-start.1 = ((bf16[64,8,128]{2,1,0:T(8,128)(2,1)}), bf16[64,8,128]{2,1,0:T(8,128)(2,1)S(1)}, u32[]{:S(2)}, u32[]{:S(2)}) async-start(bf16[64,8,128]{2,1,0:T(8,128)(2,1)} %bitcast.7), calls=%async_computation.1 | async-start | bytes 262144 | tf_op jit(solution)/shard_map/all_to_all | solution.py:116
  164.0 7.4 %all-to-all-done.1 = bf16[64,8,128]{2,1,0:T(8,128)(2,1)S(1)} async-done(((bf16[64,8,128]{2,1,0:T(8,128)(2,1)}), bf16[64,8,128]{2,1,0:T(8,128)(2,1)S(1)}, u32[]{:S(2)}, u32[]{:S(2)}) %all-to-all-start.1) | async-done | bytes 131104 | tf_op jit(solution)/shard_map/all_to_all | solution.py:116
  174.1 3.3 fusion.40
  177.4 1.3 copy.111
  178.8 1.8 copy.113
  180.5 3.3 fusion.42
  183.8 3.3 fusion.5
  187.1 4.6 %add_bitcast_fusion.1 = (f32[8,64,64,4]{1,2,3,0:T(8,128)}, f32[8,64,64,4]{1,2,3,0:T(8,128)S(1)}) fusion(f32[64,8,64,4]{2,0,3,1:T(8,128)S(1)} %fusion.5, f32[64,4]{0,1:T(4,128)S(1)} %get-tuple-element.23, f32[64,4]{0,1:T(4,128)S(1)} %get-tuple-element.22, f32[64,8,64,4]{2,0,3,1:T(8,128)S(1)} %fusion.42, f32[8,64,64,4]{2,1,3,0:T(8,128)S(1)} %copy.116), kind=kOutput, calls=%fused_computation.23 | convolution fusion | flops 101769216 | bytes 2623488 | tf_op jit(solution)/shard_map/...ab,ak->...kb/dot_general | solution.py:50
  192.1 1.9 fusion.73
  194.1 1.6 copy.122
  195.7 3.0 fusion.4
  198.8 1.5 copy.168
  200.3 1.1 reshape.139
  201.4 1.1 reshape.140
  202.6 1.3 slice.96
  203.9 1.9 fusion.71
  205.8 2.1 fusion.2
  209.2 8.9 %reverse = f32[8,16384]{1,0:T(8,128)S(1)} reverse(f32[8,16384]{1,0:T(8,128)S(1)} %bitcast.226), dimensions={1} | reverse | bytes 1048576
  218.3 9.3 %reverse.1 = f32[8,16384]{1,0:T(8,128)S(1)} reverse(f32[8,16384]{1,0:T(8,128)S(1)} %bitcast.229), dimensions={1} | reverse | bytes 1048576
  229.4 0.8 fusion.36
  230.2 0.8 convolution_add_fusion.2
  231.0 0.9 subtract_bitcast_fusion.2
  232.9 3.3 fusion.38
  236.2 1.3 copy.131
  237.5 1.8 copy.133
  239.3 3.3 fusion.44
  242.6 3.3 convolution_add_fusion
  245.9 4.6 %add_bitcast_fusion = (f32[8,64,64,4]{1,2,3,0:T(8,128)S(1)}, f32[8,64,64,4]{1,2,3,0:T(8,128)}) fusion(f32[64,8,64,4]{2,0,3,1:T(8,128)S(1)} %convolution_add_fusion, f32[64,4]{0,1:T(4,128)S(1)} %fusion.75, f32[64,4]{0,1:T(4,128)S(1)} %get-tuple-element.22, f32[64,8,64,4]{2,0,3,1:T(8,128)S(1)} %fusion.44, f32[8,64,64,4]{2,1,3,0:T(8,128)S(1)} %copy.136), kind=kOutput, calls=%fused_computation.21 | convolution fusion | flops 101638144 | bytes 2623488 | tf_op jit(solution)/shard_map/...ab,ak->...kb/dot_general | solution.py:50
  250.5 1.6 copy.141
  252.1 1.9 fusion.69
  254.5 2.0 fusion
  257.2 6.7 %copy.144 = bf16[1,8,8192]{1,0,2:T(2,128)(2,1)} copy(bf16[1,8,8192]{2,1,0:T(8,128)(2,1)S(1)} %fusion.20) | data formatting | bytes 262144 | tf_op jit(solution)/shard_map/broadcast_in_dim | solution.py:117
  264.4 45.4 %reduce = bf16[8192,8]{1,0:T(8,128)(2,1)S(1)} reduce(bf16[8192,1,8]{2,1,0:T(2,128)(2,1)} %bitcast.214, bf16[]{:T(256)} %broadcast.305), dimensions={1}, to_apply=%bitcast.178.reduce_sub_computation | reduce | bytes 262146
  309.9 2.3 reshape.170
  312.1 12.7 %all_to_all.26 = bf16[64,2,512]{2,1,0:T(2,128)(2,1)S(1)} all-to-all(bf16[64,2,512]{2,1,0:T(2,128)(2,1)S(1)} %reshape.170), channel_id=1, replica_groups=mesh['seq'=64,'mp'=4] {'seq'}, dimensions={0} | all-to-all | bytes 262144 | tf_op jit(solution)/shard_map/all_to_all | solution.py:118
  324.9 8.6 %reshape.171 = bf16[8192,1,8]{2,1,0:T(2,128)(2,1)} reshape(bf16[64,2,512]{2,1,0:T(2,128)(2,1)S(1)} %all_to_all.26) | data formatting | bytes 262144
  333.5 7.8 %copy.145 = bf16[1,8,8192]{2,1,0:T(8,128)(2,1)S(1)} copy(bf16[1,8,8192]{1,0,2:T(2,128)(2,1)} %bitcast.215) | data formatting | bytes 262144 | tf_op jit(solution)/shard_map/all_to_all | solution.py:118
  (60 shorter events, 13.7 us)
Async XLA Ops:
  6.5 135.7 %all-gather.2.cloned.1.call-start = ((), (), s32[]{:S(2)}) async-start(), calls=%async_computation.3 | async-start | bytes 12779520 | tf_op jit(solution)/shard_map/all_gather | solution.py:99
  9.4 40.3 %all-to-all-start = ((bf16[4,128,1024]{2,1,0:T(8,128)(2,1)}), bf16[4,128,1024]{2,1,0:T(8,128)(2,1)S(1)}, u32[]{:S(2)}, u32[]{:S(2)}) async-start(bf16[4,128,1024]{2,1,0:T(8,128)(2,1)} %stack.2), calls=%async_computation | async-start | bytes 2097152 | tf_op jit(solution)/shard_map/all_to_all | solution.py:95
  18.4 144.7 %copy-start.3 = (f32[8,8192]{1,0:T(8,128)S(1)}, f32[8,8192]{1,0:T(8,128)}, u32[]{:S(2)}) copy-start(f32[8,8192]{1,0:T(8,128)} %param.8) | copy-start | bytes 786436
  148.6 3.5 %collective-permute-start = (bf16[2,3,512]{2,0,1:T(2,128)(2,1)S(1)}, bf16[2,3,512]{2,0,1:T(2,128)(2,1)S(1)}, u32[]{:S(2)}, u32[]{:S(2)}) collective-permute-start(bf16[2,3,512]{2,0,1:T(2,128)(2,1)S(1)} %slice.84), channel_id=1, source_target_pairs={{0,4},{4,8},{8,12},{12,16},{16,20},{20,24},{24,28},{28,32},{32,36}... | collective-permute-start | bytes 18440 | tf_op jit(solution)/shard_map/ppermute | solution.py:11
  152.5 0.9 copy-start
  154.2 17.2 %all-to-all-start.1 = ((bf16[64,8,128]{2,1,0:T(8,128)(2,1)}), bf16[64,8,128]{2,1,0:T(8,128)(2,1)S(1)}, u32[]{:S(2)}, u32[]{:S(2)}) async-start(bf16[64,8,128]{2,1,0:T(8,128)(2,1)} %bitcast.7), calls=%async_computation.1 | async-start | bytes 262144 | tf_op jit(solution)/shard_map/all_to_all | solution.py:116
  202.6 25.2 %slice-start = ((f32[8,16384]{1,0:T(8,128)}), f32[8,1]{1,0:T(8,128)S(1)}, s32[]{:S(2)}) async-start(f32[8,16384]{1,0:T(8,128)} %reshape.140), calls=%async_computation.4 | async-start | bytes 8192 | tf_op jit(solution)/shard_map/slice | solution.py:68
  202.6 25.6 %copy-start.2 = (f32[8,64,256]{2,1,0:T(8,128)S(1)}, f32[8,64,256]{2,1,0:T(8,128)}, u32[]{:S(2)}) copy-start(f32[8,64,256]{2,1,0:T(8,128)} %reshape.139) | copy-start | bytes 1572868
  256.8 84.9 %copy-start.1 = (f32[128,3,512]{2,0,1:T(8,128)S(1)}, f32[128,3,512]{2,0,1:T(8,128)}, u32[]{:S(2)}) copy-start(f32[128,3,512]{2,0,1:T(8,128)} %copy-done) | copy-start | bytes 2359300
  256.8 84.9 %copy-start.4 = (f32[512]{0:T(512)S(1)}, f32[512]{0:T(512)}, u32[]{:S(2)}) copy-start(f32[512]{0:T(512)} %param.9) | copy-start | bytes 6148
Sparse Core Ops, SparseCore 0:
  9.2 132.9 all-gather.1
